TPU v7x, 32 devices: a whole 2x2x4 slice. The times are simulated.
32 devices in a mesh: seq: 2 (over x), ctx: 8 (over z, y), wsh: 2 (over core).
Axes of the slice: x: 2, y: 2, z: 4, core: 2. Of those that a mesh axis runs over, the one named last changes fastest.
Arguments:
- layer_in: bfloat16 [2, 1024, 896], P('seq', 'ctx'), may hold values from -6 to 6
- grad_out: bfloat16 [2, 1024, 896], P('seq', 'ctx'), may hold values from -6 to 6
- positions: int32 [2, 1024], P('seq'), may hold values from 0 to 1023, as said below
- attn_gain: bfloat16 [896], P(('seq', 'ctx', 'wsh')), may hold values from 0.099609375 to 1.8984375
- w_query: bfloat16 [896, 896], P(('seq', 'ctx'), 'wsh'), may hold values from -0.1875 to 0.1875
- b_query: bfloat16 [896], P(('seq', 'ctx', 'wsh')), may hold values from -3 to 3
- w_keyvalue: bfloat16 [896, 256], P(('seq', 'ctx'), 'wsh'), may hold values from -0.1875 to 0.1875
- b_keyvalue: bfloat16 [256], P(('seq', 'ctx', 'wsh')), may hold values from -3 to 3
- w_output: bfloat16 [896, 896], P('wsh', ('seq', 'ctx')), may hold values from -3 to 3
- mlp_gain: bfloat16 [896], P(('seq', 'ctx', 'wsh')), may hold values from 0.099609375 to 1.8984375
- w_gate: bfloat16 [896, 4864], P(('seq', 'ctx'), 'wsh'), may hold values from -0.1875 to 0.1875
- w_up: bfloat16 [896, 4864], P(('seq', 'ctx'), 'wsh'), may hold values from -0.1875 to 0.1875
- w_down: bfloat16 [4864, 896], P('wsh', ('seq', 'ctx')), may hold values from -0.078125 to 0.078125
Outputs:
- layer_out: bfloat16 [2, 1024, 896], P('seq', 'ctx')
- grad_in: bfloat16 [2, 1024, 896], P('seq', 'ctx')
- grad_attn_gain: float32 [896], P(('seq', 'ctx', 'wsh'))
- grad_w_query: float32 [896, 896], P(('seq', 'ctx'), 'wsh')
- grad_b_query: float32 [896], P(('seq', 'ctx', 'wsh'))
- grad_w_keyvalue: float32 [896, 256], P(('seq', 'ctx'), 'wsh')
- grad_b_keyvalue: float32 [256], P(('seq', 'ctx', 'wsh'))
- grad_w_output: float32 [896, 896], P('wsh', ('seq', 'ctx'))
- grad_mlp_gain: float32 [896], P(('seq', 'ctx', 'wsh'))
- grad_w_gate: float32 [896, 4864], P(('seq', 'ctx'), 'wsh')
- grad_w_up: float32 [896, 4864], P(('seq', 'ctx'), 'wsh')
- grad_w_down: float32 [4864, 896], P('wsh', ('seq', 'ctx'))
Inputs may be any that keep to these rules, and one draw needn't show every extreme that they name: Each row (one sequence) holds every position 0 to 1023 once; the 128 rows of one index of ctx are two blocks of 64 consecutive positions, block p then block 15 - p, with the pair p of each index drawn per sequence.
All inputs are finite; a program needn't handle non-finite values.
Results may differ from a plain program's by a relative error of at most 0.018.
Values may be sent and summed in bfloat16 or wider, within the bound.
No kernel may reach another device: no remote copies, remote signals or barrier semaphores. Data moves between devices by JAX's collectives and lax.ppermute only.
A program may use at most 192 MiB of HBM per device.

v0:
```python
import math
import jax
import jax.numpy as jnp
from jax import lax
from jax.sharding import PartitionSpec as P

HD = 64
epsilon = 1e-06
theta_log = math.log(1000000.0)


def partner(block, axis, stride):
    count = lax.axis_size(axis)
    route = []
    for low in range(count):
        high = low | 1 << stride
        if high != low and high < count:
            route += [(low, high), (high, low)]
    return lax.ppermute(block, axis, route)


def rope_tables(positions, half_dim):
    inv_freq = jnp.exp(-jnp.arange(half_dim, dtype=jnp.float32) * (theta_log / half_dim))
    turned = positions.astype(jnp.float32)[:, None] * inv_freq[None, :]
    return (jnp.cos(turned)[:, None, :], jnp.sin(turned)[:, None, :])


def rotate(values, cos_tab, sin_tab):
    half_dim = values.shape[-1] // 2
    first_half = values[..., :half_dim]
    second_half = values[..., half_dim:]
    return jnp.concatenate(
        [
            first_half * cos_tab - second_half * sin_tab,
            second_half * cos_tab + first_half * sin_tab,
        ],
        axis=-1,
    )


def left_inner(left_mat, right_mat):
    return lax.dot_general(
        left_mat, right_mat, (((0,), (0,)), ((), ())), preferred_element_type=jnp.float32
    )


def right_inner(left_mat, right_mat):
    return lax.dot_general(
        left_mat, right_mat, (((1,), (1,)), ((), ())), preferred_element_type=jnp.float32
    )


def norm_back(grad_normed, normed_hat, scale_inv, gain_vec):
    weighted = grad_normed * gain_vec
    return scale_inv * (
        weighted - normed_hat * jnp.mean(weighted * normed_hat, axis=-1, keepdims=True)
    )


def halve_sum(buffer, sender, group_count, group_index):
    for bit_pos in reversed(range(group_count.bit_length() - 1)):
        half_rows = buffer.shape[0] // 2
        my_bit = group_index >> bit_pos & 1
        kept_rows = lax.dynamic_slice_in_dim(buffer, my_bit * half_rows, half_rows, 0)
        outgoing = lax.dynamic_slice_in_dim(buffer, (1 - my_bit) * half_rows, half_rows, 0)
        buffer = kept_rows + sender(outgoing, bit_pos)
    return buffer


def per_device(
    layer_in,
    grad_out,
    positions,
    attn_gain,
    w_query,
    b_query,
    w_keyvalue,
    b_keyvalue,
    w_output,
    mlp_gain,
    w_gate,
    w_up,
    w_down,
):
    wq_full, wkv_full, wo_full, wg_full, wu_full, wd_full = (
        lax.all_gather(w_query, ("seq", "ctx"), axis=0, tiled=True),
        lax.all_gather(w_keyvalue, ("seq", "ctx"), axis=0, tiled=True),
        lax.all_gather(w_output, ("seq", "ctx"), axis=1, tiled=True),
        lax.all_gather(w_gate, ("seq", "ctx"), axis=0, tiled=True),
        lax.all_gather(w_up, ("seq", "ctx"), axis=0, tiled=True),
        lax.all_gather(w_down, ("seq", "ctx"), axis=1, tiled=True),
    )
    g_one, bias_q, bias_kv, g_two = (
        lax.all_gather(attn_gain, ("seq", "ctx", "wsh"), axis=0, tiled=True),
        lax.all_gather(b_query, ("seq", "ctx", "wsh"), axis=0, tiled=True),
        lax.all_gather(b_keyvalue, ("seq", "ctx", "wsh"), axis=0, tiled=True),
        lax.all_gather(mlp_gain, ("seq", "ctx", "wsh"), axis=0, tiled=True),
    )
    shard_id = lax.axis_index("wsh")
    group_count = lax.axis_size(("seq", "ctx"))
    group_index = lax.axis_index(("seq", "ctx"))
    q_cols = wq_full.shape[1]
    kv_cols = wkv_full.shape[1]
    ff_cols = wg_full.shape[1]
    bias_q = lax.dynamic_slice_in_dim(bias_q, shard_id * q_cols, q_cols).astype(jnp.float32)
    bias_kv = lax.dynamic_slice_in_dim(bias_kv, shard_id * kv_cols, kv_cols).astype(jnp.float32)
    g_one = g_one.astype(jnp.float32)
    g_two = g_two.astype(jnp.float32)
    row_count = layer_in.shape[1]
    head_count = q_cols // HD
    seq_len = positions.shape[1]
    score_scale = 1.0 / math.sqrt(HD)
    pos_all = positions[0]
    pos_mine = lax.dynamic_slice_in_dim(pos_all, lax.axis_index("ctx") * row_count, row_count)
    x_full = layer_in[0].astype(jnp.float32)
    scale_one = lax.rsqrt(jnp.mean(x_full * x_full, axis=-1, keepdims=True) + epsilon)
    hat_one = x_full * scale_one
    normed_one = (hat_one * g_one).astype(jnp.bfloat16)
    query_pre = jnp.dot(normed_one, wq_full, preferred_element_type=jnp.float32) + bias_q
    kv_pre = jnp.dot(normed_one, wkv_full, preferred_element_type=jnp.float32) + bias_kv
    cos_tab, sin_tab = rope_tables(pos_mine, HD // 2)
    query_low = rotate(query_pre.reshape(row_count, head_count, HD), cos_tab, sin_tab).astype(
        jnp.bfloat16
    )
    key_low = rotate(kv_pre[:, None, :HD], cos_tab, sin_tab)[:, 0, :].astype(jnp.bfloat16)
    value_low = kv_pre[:, HD:].astype(jnp.bfloat16)
    kv_all = lax.all_gather(
        jnp.concatenate([key_low, value_low], axis=1), "ctx", axis=0, tiled=True
    )
    k_rows = math.gcd(seq_len, 512)
    blocks_n = seq_len // k_rows
    kv_blocks = kv_all.reshape(blocks_n, k_rows, 2 * HD)
    pos_blocks = pos_all.reshape(blocks_n, k_rows)

    def block_scores(kv_block, pos_block):
        scores = (
            jnp.einsum(
                "qhd,kd->hqk", query_low, kv_block[:, :HD], preferred_element_type=jnp.float32
            )
            * score_scale
        )
        allowed = pos_block[None, :] <= pos_mine[:, None]
        return jnp.where(allowed[None], scores, -1e30)

    def stats_step(run_state, kv_pair):
        run_max, run_sum = run_state
        scores = block_scores(kv_pair[0], kv_pair[1])
        new_max = jnp.maximum(run_max, jnp.max(scores, axis=-1))
        run_sum = run_sum * jnp.exp(run_max - new_max) + jnp.sum(
            jnp.exp(scores - new_max[..., None]), axis=-1
        )
        return ((new_max, run_sum), None)

    init_max = jnp.full((head_count, row_count), -1e30, jnp.float32)
    init_sum = jnp.zeros((head_count, row_count), jnp.float32)
    (run_max, run_sum), unused = lax.scan(stats_step, (init_max, init_sum), (kv_blocks, pos_blocks))
    log_sum = run_max + jnp.log(run_sum)

    def out_step(run_state, kv_pair):
        sum_low, sum_full = run_state
        scores = block_scores(kv_pair[0], kv_pair[1])
        prob_full = jnp.exp(scores - log_sum[..., None])
        prob_low = prob_full.astype(jnp.bfloat16)
        value_blk = kv_pair[0][:, HD:]
        sum_low = sum_low + jnp.einsum(
            "hqk,kd->hqd", prob_low, value_blk, preferred_element_type=jnp.float32
        )
        sum_full = sum_full + jnp.einsum(
            "hqk,kd->hqd",
            prob_full,
            value_blk.astype(jnp.float32),
            preferred_element_type=jnp.float32,
        )
        return ((sum_low, sum_full), None)

    zero_heads = jnp.zeros((head_count, row_count, HD), jnp.float32)
    (attended, attended_exact), unused = lax.scan(
        out_step, (zero_heads, zero_heads), (kv_blocks, pos_blocks)
    )
    attended_low = (
        jnp.transpose(attended, (1, 0, 2)).reshape(row_count, head_count * HD).astype(jnp.bfloat16)
    )
    branch = lax.psum(jnp.dot(attended_low, wo_full, preferred_element_type=jnp.float32), "wsh")
    hidden = x_full + branch
    scale_two = lax.rsqrt(jnp.mean(hidden * hidden, axis=-1, keepdims=True) + epsilon)
    hat_two = hidden * scale_two
    normed_two = (hat_two * g_two).astype(jnp.bfloat16)
    gate_pre = jnp.dot(normed_two, wg_full, preferred_element_type=jnp.float32)
    up_proj = jnp.dot(normed_two, wu_full, preferred_element_type=jnp.float32)
    act_low = (jax.nn.silu(gate_pre) * up_proj).astype(jnp.bfloat16)
    mlp_out = lax.psum(
        jnp.dot(act_low, wd_full, preferred_element_type=jnp.float32).astype(jnp.bfloat16), "wsh"
    ).astype(jnp.float32)
    layer_out = (hidden + mlp_out).astype(jnp.bfloat16)
    wq_full, wkv_full, wo_full, wg_full, wu_full, wd_full = (
        lax.all_gather(w_query, ("seq", "ctx"), axis=0, tiled=True),
        lax.all_gather(w_keyvalue, ("seq", "ctx"), axis=0, tiled=True),
        lax.all_gather(w_output, ("seq", "ctx"), axis=1, tiled=True),
        lax.all_gather(w_gate, ("seq", "ctx"), axis=0, tiled=True),
        lax.all_gather(w_up, ("seq", "ctx"), axis=0, tiled=True),
        lax.all_gather(w_down, ("seq", "ctx"), axis=1, tiled=True),
    )
    grad_low = grad_out[0]
    grad_full = grad_low.astype(jnp.float32)
    grad_act = right_inner(grad_low, wd_full)
    gw_down_t = left_inner(grad_low, act_low)
    sigmoid_g = jax.nn.sigmoid(gate_pre)
    grad_up = (grad_act * (gate_pre * sigmoid_g)).astype(jnp.bfloat16)
    grad_gate = (grad_act * up_proj * sigmoid_g * (1.0 + gate_pre * (1.0 - sigmoid_g))).astype(
        jnp.bfloat16
    )
    gw_gate = left_inner(normed_two, grad_gate)
    gw_up = left_inner(normed_two, grad_up)
    part_two = right_inner(grad_gate, wg_full) + right_inner(grad_up, wu_full)
    gg_two = jnp.sum(part_two * hat_two, axis=0)
    grad_normed_two = lax.psum(part_two.astype(jnp.bfloat16), "wsh").astype(jnp.float32)
    grad_hidden = grad_full + norm_back(grad_normed_two, hat_two, scale_two, g_two)
    hidden_low = grad_hidden.astype(jnp.bfloat16)
    gw_out_t = left_inner(hidden_low, attended_low)
    grad_att = (
        right_inner(hidden_low, wo_full).reshape(row_count, head_count, HD).astype(jnp.bfloat16)
    )
    row_delta = jnp.sum(
        jnp.transpose(grad_att.astype(jnp.float32), (1, 0, 2)) * attended_exact, axis=-1
    )

    def back_step(grad_q, kv_pair):
        kv_block, pos_block = kv_pair
        scores = block_scores(kv_block, pos_block)
        prob_full = jnp.exp(scores - log_sum[..., None])
        prob_low = prob_full.astype(jnp.bfloat16)
        grad_prob = jnp.einsum(
            "qhd,kd->hqk", grad_att, kv_block[:, HD:], preferred_element_type=jnp.float32
        )
        grad_score = (prob_full * (grad_prob - row_delta[..., None])).astype(jnp.bfloat16)
        grad_q = grad_q + jnp.einsum(
            "hqk,kd->qhd", grad_score, kv_block[:, :HD], preferred_element_type=jnp.float32
        )
        grad_key = jnp.einsum(
            "hqk,qhd->kd", grad_score, query_low, preferred_element_type=jnp.float32
        )
        grad_value = jnp.einsum(
            "hqk,qhd->kd", prob_low, grad_att, preferred_element_type=jnp.float32
        )
        return (grad_q, jnp.concatenate([grad_key * score_scale, grad_value], axis=1))

    grad_q, kv_terms = lax.scan(
        back_step, jnp.zeros((row_count, head_count, HD), jnp.float32), (kv_blocks, pos_blocks)
    )
    grad_q = grad_q * score_scale
    grad_kv = lax.psum_scatter(
        kv_terms.reshape(seq_len, 2 * HD).astype(jnp.bfloat16),
        "ctx",
        scatter_dimension=0,
        tiled=True,
    ).astype(jnp.float32)
    grad_qpre = (
        rotate(grad_q, cos_tab, -sin_tab).reshape(row_count, head_count * HD).astype(jnp.bfloat16)
    )
    grad_kpre = rotate(grad_kv[:, None, :HD], cos_tab, -sin_tab)[:, 0, :]
    grad_kvpre = jnp.concatenate([grad_kpre, grad_kv[:, HD:]], axis=1).astype(jnp.bfloat16)
    gw_query = left_inner(normed_one, grad_qpre)
    gw_kv = left_inner(normed_one, grad_kvpre)
    wsh_count = lax.axis_size("wsh")
    gb_q_full = lax.dynamic_update_slice_in_dim(
        jnp.zeros((q_cols * wsh_count,), jnp.float32),
        jnp.sum(grad_qpre.astype(jnp.float32), axis=0),
        shard_id * q_cols,
        0,
    )
    gb_kv_full = lax.dynamic_update_slice_in_dim(
        jnp.zeros((kv_cols * wsh_count,), jnp.float32),
        jnp.sum(grad_kvpre.astype(jnp.float32), axis=0),
        shard_id * kv_cols,
        0,
    )
    part_one = right_inner(grad_qpre, wq_full) + right_inner(grad_kvpre, wkv_full)
    gg_one = jnp.sum(part_one * hat_one, axis=0)
    grad_normed_one = lax.psum(part_one.astype(jnp.bfloat16), "wsh").astype(jnp.float32)
    grad_input = (grad_hidden + norm_back(grad_normed_one, hat_one, scale_one, g_one)).astype(
        jnp.bfloat16
    )
    out_g_one, out_b_q, out_b_kv, out_g_two = (
        lax.psum_scatter(gg_one, ("seq", "ctx", "wsh"), scatter_dimension=0, tiled=True),
        lax.psum_scatter(gb_q_full, ("seq", "ctx", "wsh"), scatter_dimension=0, tiled=True),
        lax.psum_scatter(gb_kv_full, ("seq", "ctx", "wsh"), scatter_dimension=0, tiled=True),
        lax.psum_scatter(gg_two, ("seq", "ctx", "wsh"), scatter_dimension=0, tiled=True),
    )
    all_owned = lax.psum_scatter(
        jnp.concatenate([gw_query, gw_kv, gw_out_t, gw_gate, gw_up, gw_down_t], axis=1).astype(
            jnp.bfloat16
        ),
        ("seq", "ctx"),
        scatter_dimension=0,
        tiled=True,
    ).astype(jnp.float32)
    proj_owned = all_owned[:, : 2 * q_cols + kv_cols]
    mlp_owned = all_owned[:, 2 * q_cols + kv_cols :]
    out_wq = proj_owned[:, :q_cols]
    out_wkv = proj_owned[:, q_cols : q_cols + kv_cols]
    out_wo = jnp.transpose(proj_owned[:, q_cols + kv_cols :])
    out_wg = mlp_owned[:, :ff_cols]
    out_wu = mlp_owned[:, ff_cols : 2 * ff_cols]
    out_wd = jnp.transpose(mlp_owned[:, 2 * ff_cols :])
    return (
        layer_out[None],
        grad_input[None],
        out_g_one,
        out_wq,
        out_b_q,
        out_wkv,
        out_b_kv,
        out_wo,
        out_g_two,
        out_wg,
        out_wu,
        out_wd,
    )


def solution(mesh):
    return jax.shard_map(
        per_device,
        mesh=mesh,
        in_specs=(
            P("seq", "ctx", None),
            P("seq", "ctx", None),
            P("seq", None),
            P(("seq", "ctx", "wsh")),
            P(("seq", "ctx"), "wsh"),
            P(("seq", "ctx", "wsh")),
            P(("seq", "ctx"), "wsh"),
            P(("seq", "ctx", "wsh")),
            P("wsh", ("seq", "ctx")),
            P(("seq", "ctx", "wsh")),
            P(("seq", "ctx"), "wsh"),
            P(("seq", "ctx"), "wsh"),
            P("wsh", ("seq", "ctx")),
        ),
        out_specs=(
            P("seq", "ctx", None),
            P("seq", "ctx", None),
            P(("seq", "ctx", "wsh")),
            P(("seq", "ctx"), "wsh"),
            P(("seq", "ctx", "wsh")),
            P(("seq", "ctx"), "wsh"),
            P(("seq", "ctx", "wsh")),
            P("wsh", ("seq", "ctx")),
            P(("seq", "ctx", "wsh")),
            P(("seq", "ctx"), "wsh"),
            P(("seq", "ctx"), "wsh"),
            P("wsh", ("seq", "ctx")),
        ),
        check_vma=False,
    )
```

profile of v0, /device:TPU:0, one launch (start us, length us, event | category | flops | bytes accessed | tf_op | source)
XLA Modules:
  0.0 914.5 jit_solution(13022958622151075140)
XLA Ops:
  12.6 42.1 %all-reduce.10 = (bf16[256]{0:T(256)(128)(2,1)S(1)}, bf16[896]{0:T(1024)(128)(2,1)S(1)}, bf16[896]{0:T(1024)(128)(2,1)S(1)}, bf16[896]{0:T(1024)(128)(2,1)S(1)}) all-reduce(bf16[256]{0:T(256)(128)(2,1)S(1)} %dynamic-update-slice.1, bf16[896]{0:T(1024)(128)(2,1)S(1)} %dynamic-update-slice, ...), channel_id=1, replica_groups=mesh['seq'=2,'ctx'=8,'wsh'=2] {'seq','ctx','wsh'}, use_global_device_ids=true, to_apply=%add.1 | all-reduce | flops 2944 | bytes 11776
  54.7 41.0 %all_gather.40 = bf16[896,128]{1,0:T(8,128)(2,1)S(1)} all-gather(bf16[56,128]{1,0:T(8,128)(2,1)} %param.25), channel_id=1, replica_groups=mesh['seq'=2,'ctx'=8,'wsh'=2] {'seq','ctx'}, dimensions={0}, use_global_device_ids=true | all-gather | bytes 243712 | tf_op jit(solution)/shard_map/all_gather | solution.py:87
  99.9 26.7 %all_gather.42 = bf16[1024,128]{0,1:T(8,128)(2,1)S(1)} all-gather(bf16[128,128]{0,1:T(8,128)(2,1)S(1)} %pad_maximum_fusion.1), channel_id=1, replica_groups=mesh['seq'=2,'ctx'=8,'wsh'=2] {'ctx'}, dimensions={0}, use_global_device_ids=true | all-gather | bytes 294912 | tf_op jit(solution)/shard_map/all_gather | solution.py:127
  126.6 42.1 %all_gather.43 = bf16[896,448]{1,0:T(8,128)(2,1)S(1)} all-gather(bf16[56,448]{1,0:T(8,128)(2,1)S(1)} %copy-done.17), channel_id=1, replica_groups=mesh['seq'=2,'ctx'=8,'wsh'=2] {'seq','ctx'}, dimensions={0}, use_global_device_ids=true | all-gather | bytes 852992 | tf_op jit(solution)/shard_map/all_gather | solution.py:86
  171.6 2.9 while.40
  174.6 42.6 %all_gather.45 = bf16[448,896]{0,1:T(8,128)(2,1)S(1)} all-gather(bf16[448,56]{0,1:T(8,128)(2,1)S(1)} %copy-done.18), channel_id=1, replica_groups=mesh['seq'=2,'ctx'=8,'wsh'=2] {'seq','ctx'}, dimensions={1}, use_global_device_ids=true | all-gather | bytes 852992 | tf_op jit(solution)/shard_map/all_gather | solution.py:88
  220.3 13.9 %all-reduce.16.cloned.1.call-done = f32[128,896]{1,0:T(8,128)} async-done(((f32[128,896]{1,0:T(8,128)}), f32[128,896]{1,0:T(8,128)}) %all-reduce.16.cloned.1.call-update) | async-done | bytes 458768 | tf_op jit(solution)/shard_map/psum | solution.py:183
  235.5 60.1 %all-gather.6.cloned.1.call-done = bf16[896,2432]{1,0:T(8,128)(2,1)} async-done(((bf16[56,2432]{1,0:T(8,128)(2,1)}), bf16[896,2432]{1,0:T(8,128)(2,1)}) %all-gather.6.cloned.1.call-update) | async-done | bytes 4358160 | tf_op jit(solution)/shard_map/all_gather | solution.py:90
  295.5 4.1 fusion.76
  299.7 73.9 %all-gather.4.cloned.1.call-done = bf16[896,2432]{1,0:T(8,128)(2,1)} async-done(((bf16[56,2432]{1,0:T(8,128)(2,1)}), bf16[896,2432]{1,0:T(8,128)(2,1)}) %all-gather.4.cloned.1.call-update) | async-done | bytes 4358160 | tf_op jit(solution)/shard_map/all_gather | solution.py:89
  373.6 4.1 fusion.75
  377.7 73.9 %all-gather.8.cloned.1.call-done = bf16[2432,896]{0,1:T(8,128)(2,1)} async-done(((bf16[2432,56]{0,1:T(8,128)(2,1)}), bf16[2432,896]{0,1:T(8,128)(2,1)}) %all-gather.8.cloned.1.call-update) | async-done | bytes 4358160 | tf_op jit(solution)/shard_map/all_gather | solution.py:91
  451.6 5.0 multiply_convert_fusion
  456.6 3.4 convolution_convert_fusion.1
  461.3 4.4 fusion.72
  466.0 4.6 fusion.14
  470.6 4.4 convolution_convert_fusion.6
  474.9 3.5 convolution_convert_fusion.2
  478.4 4.2 all-reduce.18.cloned.1.call-done
  487.1 6.6 while.41
  498.4 60.5 %reduce-scatter.8.cloned.1.call-done = bf16[128,128]{1,0:T(8,128)(2,1)} async-done(((bf16[1024,128]{1,0:T(8,128)(2,1)}), bf16[128,128]{1,0:T(8,128)(2,1)}) %reduce-scatter.8.cloned.1.call-update) | async-done | bytes 32784
  565.7 25.7 %concatenate.35 = bf16[896,8320]{1,0:T(8,128)(2,1)} concatenate(bf16[896,448]{1,0:T(8,128)(2,1)S(1)} %copy.48, bf16[896,128]{1,0:T(8,128)(2,1)S(1)} %copy.49, bf16[896,448]{1,0:T(8,128)(2,1)S(1)} %copy.50, bf16[896,2432]{1,0:T(8,128)(2,1)} %convolution_convert_fusion.2, bf16[896,2432]{1,0:T(8,128)(2,1)} %convolution_convert_fusion.1, bf16[896,2432]{1,0:T(8,128)(2,1)} %fusion.14), dimensions={1} | concatenate | bytes 29818880 | tf_op jit(solution)/shard_map/concatenate | solution.py:290
  593.6 68.7 %all-reduce.9 = (f32[896]{0:T(1024)S(1)}, f32[896]{0:T(1024)S(1)}, f32[256]{0:T(256)S(1)}, f32[896]{0:T(1024)S(1)}) all-reduce(f32[896]{0:T(1024)S(1)} %get-tuple-element.288, f32[896]{0:T(1024)S(1)} %dynamic_update_slice.10, f32[256]{0:T(256)S(1)} %dynamic_update_slice.11, ...), channel_id=3, replica_groups=mesh['seq'=2,'ctx'=8,'wsh'=2] {'seq','ctx','wsh'}, use_global_device_ids=true, to_apply=%region_19.20.clone | all-reduce | flops 2944 | bytes 23552
  666.6 235.9 %reduce-scatter.10.cloned.1.call-done = bf16[56,8320]{1,0:T(8,128)(2,1)} async-done(((bf16[896,8320]{1,0:T(8,128)(2,1)}), bf16[56,8320]{1,0:T(8,128)(2,1)}) %reduce-scatter.10.cloned.1.call-update) | async-done | bytes 931856
  (190 shorter events, 55.7 us)
Async XLA Ops:
  8.0 160.8 %copy-start.1 = (bf16[1,128,896]{2,1,0:T(8,128)(2,1)S(1)}, bf16[1,128,896]{2,1,0:T(8,128)(2,1)}, u32[]{:S(2)}) copy-start(bf16[1,128,896]{2,1,0:T(8,128)(2,1)} %param.19) | copy-start | bytes 688132
  8.0 118.6 %copy-start.17 = (bf16[56,448]{1,0:T(8,128)(2,1)S(1)}, bf16[56,448]{1,0:T(8,128)(2,1)}, u32[]{:S(2)}) copy-start(bf16[56,448]{1,0:T(8,128)(2,1)} %param.23) | copy-start | bytes 150532
  8.0 226.2 %all-reduce.16.cloned.1.call-start = ((), (), s32[]{:S(2)}) async-start(), calls=%async_computation.2 | async-start | bytes 917504 | tf_op jit(solution)/shard_map/psum | solution.py:183
  95.6 31.0 %copy-start.13 = (bf16[896,128]{1,0:T(8,128)(2,1)}, bf16[896,128]{1,0:T(8,128)(2,1)S(1)}, u32[]{:S(2)}) copy-start(bf16[896,128]{1,0:T(8,128)(2,1)S(1)} %all_gather.40) | copy-start | bytes 688132
  171.6 3.0 copy-start.18
  174.5 45.1 %copy-start.2 = (f32[7,128,64]{1,2,0:T(8,128)}, f32[7,128,64]{1,2,0:T(8,128)S(1)}, u32[]{:S(2)}) copy-start(f32[7,128,64]{1,2,0:T(8,128)S(1)} %get-tuple-element.149) | copy-start | bytes 688132
  174.6 45.6 %copy-start.11 = (bf16[7,128,64]{1,2,0:T(8,128)(2,1)}, bf16[7,128,64]{1,2,0:T(8,128)(2,1)S(1)}, u32[]{:S(2)}) copy-start(bf16[7,128,64]{1,2,0:T(8,128)(2,1)S(1)} %convert_element_type.151) | copy-start | bytes 344068
  218.4 77.1 %all-gather.6.cloned.1.call-start = ((), (), s32[]{:S(2)}) async-start(), calls=%async_computation.4 | async-start | bytes 4630528 | tf_op jit(solution)/shard_map/all_gather | solution.py:90
  219.0 154.6 %all-gather.4.cloned.1.call-start = ((), (), s32[]{:S(2)}) async-start(), calls=%async_computation.3 | async-start | bytes 4630528 | tf_op jit(solution)/shard_map/all_gather | solution.py:89
  219.6 232.0 %all-gather.8.cloned.1.call-start = ((), (), s32[]{:S(2)}) async-start(), calls=%async_computation.5 | async-start | bytes 4630528 | tf_op jit(solution)/shard_map/all_gather | solution.py:91
  220.2 262.4 %all-reduce.18.cloned.1.call-start = ((), (), s32[]{:S(2)}) async-start(), calls=%async_computation.6 | async-start | bytes 458752 | tf_op jit(solution)/shard_map/psum | solution.py:216
  456.6 3.4 copy-start.8
  456.6 3.4 copy-start
  465.7 93.2 %reduce-scatter.8.cloned.1.call-start = ((), (), s32[]{:S(2)}) async-start(), calls=%async_computation.7 | async-start | bytes 294912
  465.9 4.6 copy-start.7
  470.6 4.4 copy-start.9
  482.6 3.1 copy-start.12
  484.0 3.1 copy-start.3
  485.3 1.8 copy-start.4
  495.5 96.6 %all-reduce.20.cloned.1.call-start = ((), (), s32[]{:S(2)}) async-start(), calls=%async_computation.9 | async-start | bytes 917504 | tf_op jit(solution)/shard_map/psum | solution.py:191
  495.5 64.7 %copy-start.14 = (bf16[896,128]{1,0:T(8,128)(2,1)S(1)}, bf16[896,128]{1,0:T(8,128)(2,1)}, u32[]{:S(2)}) copy-start(bf16[896,128]{1,0:T(8,128)(2,1)} %copy-done.13) | copy-start | bytes 688132
  562.4 340.1 %reduce-scatter.10.cloned.1.call-start = ((), (), s32[]{:S(2)}) async-start(), calls=%async_computation.8 | async-start | bytes 15841280
  591.4 73.2 %copy-start.5 = (f32[128,896]{1,0:T(8,128)S(1)}, f32[128,896]{1,0:T(8,128)}, u32[]{:S(2)}) copy-start(f32[128,896]{1,0:T(8,128)} %copy-done.4) | copy-start | bytes 1376260
  902.5 2.1 copy-start.6
  (5 other events, 4.3 us)
Sparse Core Ops, SparseCore 0:
  218.5 15.6 all-reduce.15
  465.8 16.7 all-reduce.17
  495.6 63.3 reduce-scatter.7
  562.5 17.6 all-reduce.19
Sparse Core Ops, SparseCore 1:
  221.7 73.8 all-gather.5
  298.2 75.3 all-gather.3
  376.3 75.3 all-gather.7
  591.5 310.9 reduce-scatter.9
where the time goes:
time: 916 us; the launch traced here: 915 us
  waiting for transfers between devices  524 us (57%)
  blocking collectives  263 us (29%)
  matrix products  52 us (6%)
  local copies, waits for them, and re-layouts  44.2 us (5%)
  between operations  16 us (2%)
  other arithmetic  14.3 us (2%)
    unnamed x10, waiting for transfers between devices  298 us
    unnamed x2, blocking collectives  111 us
    all_gather x1, waiting for transfers between devices, per_device(): lax.all_gather(w_down, ('seq', 'ctx'), axis=1, tiled=True)  73.9 us
    all_gather x1, waiting for transfers between devices, per_device(): lax.all_gather(w_gate, ('seq', 'ctx'), axis=0, tiled=True)  73.9 us
    all_gather x1, waiting for transfers between devices, per_device(): lax.all_gather(w_up, ('seq', 'ctx'), axis=0, tiled=True)  60.1 us
    all_gather x1, blocking collectives, per_device(): lax.all_gather(w_output, ('seq', 'ctx'), axis=1, tiled=True)  42.6 us
    all_gather x1, blocking collectives, per_device(): lax.all_gather(w_query, ('seq', 'ctx'), axis=0, tiled=True)  42.1 us
    all_gather x1, blocking collectives, per_device(): lax.all_gather(w_keyvalue, ('seq', 'ctx'), axis=0, tiled=True)  41 us
  transfers between devices with their start and end apart: 8, of which 7 were waited for; matrix products, arithmetic and copies ran while one was open for 7% of the time, Pallas kernels for 0%

commit v1 on v0

--- a/solution.py
+++ b/solution.py
@@ -1,3 +1,4 @@
+import functools
 import math
 import jax
 import jax.numpy as jnp
@@ -7,6 +8,30 @@
 HD = 64
 epsilon = 1e-06
 theta_log = math.log(1000000.0)
+
+
+def get_pipes(block_here, chip_axis):
+    h_now = lax.axis_size(chip_axis)
+    step_out = lax.axis_index(chip_axis)
+    block_last, arr_now, passed = (h_now, step_out, block_here.shape[1])
+    local_next, found_now = (block_here, 1)
+    while found_now < block_last:
+        local_next = jnp.concatenate(
+            [
+                local_next,
+                lax.ppermute(
+                    local_next,
+                    chip_axis,
+                    list(map(lambda h: (h, (h - found_now) % block_last), range(block_last))),
+                ),
+            ],
+            axis=1,
+        )
+        found_now = 2 * found_now
+    return jnp.roll(local_next, arr_now * passed, axis=1)
+
+
+treat_task_in = functools.partial(get_pipes, chip_axis=("seq", "ctx"))
 
 
 def partner(block, axis, stride):
@@ -88,7 +113,7 @@
         lax.all_gather(w_output, ("seq", "ctx"), axis=1, tiled=True),
         lax.all_gather(w_gate, ("seq", "ctx"), axis=0, tiled=True),
         lax.all_gather(w_up, ("seq", "ctx"), axis=0, tiled=True),
-        lax.all_gather(w_down, ("seq", "ctx"), axis=1, tiled=True),
+        treat_task_in(w_down),
     )
     g_one, bias_q, bias_kv, g_two = (
         lax.all_gather(attn_gain, ("seq", "ctx", "wsh"), axis=0, tiled=True),

time: 916 us -> 960 us (1.048)
  waiting for transfers between devices: 524 us -> 547 us
  local copies, waits for them, and re-layouts: 44.2 us -> 61.8 us
    ppermute x0 -> x4, waiting for transfers between devices: none -> 103 us  [get_pipes(): lax.ppermute(local_next, chip_axis, list(map(lambda h: (h, (h - found_now...]
    all_gather x1, waiting for transfers between devices: 73.9 us -> 0.01 us  [per_device(): lax.all_gather(w_gate, ('seq', 'ctx'), axis=0, tiled=True)]
    psum x1, waiting for transfers between devices: 13.9 us -> 0.01 us  [per_device(): lax.psum(jnp.dot(attended_low, wo_full, preferred_element_type=jnp.float3...]
    unnamed x50 -> x101, local copies, waits for them, and re-layouts: 8.59 us -> 18.3 us
  transfers between devices with their start and end apart: 8 -> 12, of which waited for: 7 -> 9; matrix products, arithmetic and copies ran while one was open for 7% -> 8% of each run, Pallas kernels for 0% -> 0%
where the time goes in v1:
time: 960 us; the launch traced here: 958 us
  waiting for transfers between devices  547 us (57%)
  blocking collectives  262 us (27%)
  local copies, waits for them, and re-layouts  61.8 us (6%)
  matrix products  50 us (5%)
  other arithmetic  16.7 us (2%)
  between operations  16.2 us (2%)
    unnamed x10, waiting for transfers between devices  298 us
    unnamed x2, blocking collectives  108 us
    ppermute x4, waiting for transfers between devices, get_pipes(): lax.ppermute(local_next, chip_axis, list(map(lambda h: (h, (h - found_now...  103 us
    all_gather x1, waiting for transfers between devices, per_device(): lax.all_gather(w_down, ('seq', 'ctx'), axis=1, tiled=True)  73.9 us
    all_gather x1, waiting for transfers between devices, per_device(): lax.all_gather(w_up, ('seq', 'ctx'), axis=0, tiled=True)  63.1 us
    all_gather x1, blocking collectives, per_device(): lax.all_gather(w_output, ('seq', 'ctx'), axis=1, tiled=True)  44.1 us
    all_gather x1, blocking collectives, per_device(): lax.all_gather(w_query, ('seq', 'ctx'), axis=0, tiled=True)  41.7 us
    all_gather x1, blocking collectives, per_device(): lax.all_gather(w_keyvalue, ('seq', 'ctx'), axis=0, tiled=True)  41.2 us
  transfers between devices with their start and end apart: 12, of which 9 were waited for; matrix products, arithmetic and copies ran while one was open for 8% of the time, Pallas kernels for 0%

profile of v1, /device:TPU:0, one launch (start us, length us, event | category | flops | bytes accessed | tf_op | source)
XLA Modules:
  0.0 957.9 jit_solution(2432339278425962991)
XLA Ops:
  11.5 42.1 %all-reduce.10 = (bf16[256]{0:T(256)(128)(2,1)S(1)}, bf16[896]{0:T(1024)(128)(2,1)S(1)}, bf16[896]{0:T(1024)(128)(2,1)S(1)}, bf16[896]{0:T(1024)(128)(2,1)}) all-reduce(bf16[256]{0:T(256)(128)(2,1)S(1)} %dynamic-update-slice.1, bf16[896]{0:T(1024)(128)(2,1)S(1)} %dynamic-update-slice, ...), channel_id=1, replica_groups=mesh['seq'=2,'ctx'=8,'wsh'=2] {'seq','ctx','wsh'}, use_global_device_ids=true, to_apply=%add.1 | all-reduce | flops 2944 | bytes 11776
  54.7 41.2 %all_gather.39 = bf16[896,128]{1,0:T(8,128)(2,1)S(1)} all-gather(bf16[56,128]{1,0:T(8,128)(2,1)} %param.25), channel_id=1, replica_groups=mesh['seq'=2,'ctx'=8,'wsh'=2] {'seq','ctx'}, dimensions={0}, use_global_device_ids=true | all-gather | bytes 243712 | tf_op jit(solution)/shard_map/all_gather | solution.py:112
  98.9 26.7 %all_gather.41 = bf16[1024,128]{0,1:T(8,128)(2,1)S(1)} all-gather(bf16[128,128]{0,1:T(8,128)(2,1)S(1)} %pad_maximum_fusion.4), channel_id=1, replica_groups=mesh['seq'=2,'ctx'=8,'wsh'=2] {'ctx'}, dimensions={0}, use_global_device_ids=true | all-gather | bytes 294912 | tf_op jit(solution)/shard_map/all_gather | solution.py:152
  125.6 41.7 %all_gather.42 = bf16[896,448]{1,0:T(8,128)(2,1)S(1)} all-gather(bf16[56,448]{1,0:T(8,128)(2,1)S(1)} %copy-done.24), channel_id=1, replica_groups=mesh['seq'=2,'ctx'=8,'wsh'=2] {'seq','ctx'}, dimensions={0}, use_global_device_ids=true | all-gather | bytes 852992 | tf_op jit(solution)/shard_map/all_gather | solution.py:111
  169.9 3.5 while.39
  173.5 6.6 while.40
  180.1 44.1 %all_gather.44 = bf16[448,896]{0,1:T(8,128)(2,1)S(1)} all-gather(bf16[448,56]{0,1:T(8,128)(2,1)S(1)} %copy-done.25), channel_id=1, replica_groups=mesh['seq'=2,'ctx'=8,'wsh'=2] {'seq','ctx'}, dimensions={1}, use_global_device_ids=true | all-gather | bytes 852992 | tf_op jit(solution)/shard_map/all_gather | solution.py:113
  228.7 5.5 collective-permute-done
  234.9 21.3 %collective-permute-done.1 = bf16[2432,112]{0,1:T(8,128)(2,1)S(1)} collective-permute-done((bf16[2432,112]{0,1:T(8,128)(2,1)S(1)}, bf16[2432,112]{0,1:T(8,128)(2,1)S(1)}, u32[]{:S(2)}, u32[]{:S(2)}) %collective-permute-start.1) | collective-permute-done | bytes 544800 | tf_op jit(solution)/shard_map/ppermute | solution.py:22
  256.8 39.2 %collective-permute-done.2 = bf16[2432,224]{0,1:T(8,128)(2,1)S(1)} collective-permute-done((bf16[2432,224]{0,1:T(8,128)(2,1)S(1)}, bf16[2432,224]{0,1:T(8,128)(2,1)S(1)}, u32[]{:S(2)}, u32[]{:S(2)}) %collective-permute-start.2) | collective-permute-done | bytes 1089568 | tf_op jit(solution)/shard_map/ppermute | solution.py:22
  303.7 36.7 %collective-permute-done.3 = bf16[2432,448]{0,1:T(8,128)(2,1)} collective-permute-done((bf16[2432,448]{0,1:T(8,128)(2,1)}, bf16[2432,448]{0,1:T(8,128)(2,1)}, u32[]{:S(2)}, u32[]{:S(2)}) %collective-permute-start.3) | collective-permute-done | bytes 2179104 | tf_op jit(solution)/shard_map/ppermute | solution.py:22
  350.2 4.2 fusion.81
  354.4 63.1 %all-gather.6.cloned.1.call-done = bf16[896,2432]{1,0:T(8,128)(2,1)} async-done(((bf16[56,2432]{1,0:T(8,128)(2,1)}), bf16[896,2432]{1,0:T(8,128)(2,1)}) %all-gather.6.cloned.1.call-update) | async-done | bytes 4358160 | tf_op jit(solution)/shard_map/all_gather | solution.py:115
  417.4 4.1 fusion.82
  421.6 73.9 %all-gather.8.cloned.1.call-done = bf16[2432,896]{0,1:T(8,128)(2,1)} async-done(((bf16[2432,56]{0,1:T(8,128)(2,1)}), bf16[2432,896]{0,1:T(8,128)(2,1)}) %all-gather.8.cloned.1.call-update) | async-done | bytes 4358160 | tf_op jit(solution)/shard_map/all_gather | solution.py:226
  495.5 4.1 multiply_convert_fusion
  499.6 3.6 convolution_convert_fusion.1
  513.8 4.3 fusion.18
  518.1 8.8 all-reduce.18.cloned.1.call-done
  531.0 6.1 while.41
  543.1 58.4 %reduce-scatter.8.cloned.1.call-done = bf16[128,128]{1,0:T(8,128)(2,1)} async-done(((bf16[1024,128]{1,0:T(8,128)(2,1)}), bf16[128,128]{1,0:T(8,128)(2,1)}) %reduce-scatter.8.cloned.1.call-update) | async-done | bytes 32784
  608.8 26.1 %concatenate.57 = bf16[896,8320]{1,0:T(8,128)(2,1)} concatenate(bf16[896,448]{1,0:T(8,128)(2,1)S(1)} %copy-done.10, bf16[896,128]{1,0:T(8,128)(2,1)S(1)} %copy.49, bf16[896,448]{1,0:T(8,128)(2,1)} %copy.50, bf16[896,2432]{1,0:T(8,128)(2,1)} %convolution_convert_fusion.2, bf16[896,2432]{1,0:T(8,128)(2,1)} %convolution_convert_fusion.1, bf16[896,2432]{1,0:T(8,128)(2,1)} %fusion.14), dimensions={1} | concatenate | bytes 29818880 | tf_op jit(solution)/shard_map/concatenate | solution.py:315
  636.7 65.9 %all-reduce.9 = (f32[896]{0:T(1024)S(1)}, f32[896]{0:T(1024)S(1)}, f32[256]{0:T(256)S(1)}, f32[896]{0:T(1024)S(1)}) all-reduce(f32[896]{0:T(1024)S(1)} %get-tuple-element.288, f32[896]{0:T(1024)S(1)} %dynamic_update_slice.10, f32[256]{0:T(256)S(1)} %dynamic_update_slice.11, ...), channel_id=3, replica_groups=mesh['seq'=2,'ctx'=8,'wsh'=2] {'seq','ctx','wsh'}, use_global_device_ids=true, to_apply=%region_19.20.clone | all-reduce | flops 2944 | bytes 23552
  707.0 238.8 %reduce-scatter.10.cloned.1.call-done = bf16[56,8320]{1,0:T(8,128)(2,1)} async-done(((bf16[896,8320]{1,0:T(8,128)(2,1)}), bf16[56,8320]{1,0:T(8,128)(2,1)}) %reduce-scatter.10.cloned.1.call-update) | async-done | bytes 931856
  (247 shorter events, 87.5 us)
Async XLA Ops:
  8.0 161.2 %copy-start = (bf16[1,128,896]{2,1,0:T(8,128)(2,1)S(1)}, bf16[1,128,896]{2,1,0:T(8,128)(2,1)}, u32[]{:S(2)}) copy-start(bf16[1,128,896]{2,1,0:T(8,128)(2,1)} %param.19) | copy-start | bytes 688132
  8.0 159.9 %copy-start.30 = (s32[1,1024]{1,0:T(1,128)S(1)}, s32[1,1024]{1,0:T(1,128)}, u32[]{:S(2)}) copy-start(s32[1,1024]{1,0:T(1,128)} %param.21) | copy-start | bytes 12292
  8.0 117.6 %copy-start.24 = (bf16[56,448]{1,0:T(8,128)(2,1)S(1)}, bf16[56,448]{1,0:T(8,128)(2,1)}, u32[]{:S(2)}) copy-start(bf16[56,448]{1,0:T(8,128)(2,1)} %param.23) | copy-start | bytes 150532
  8.0 292.4 %all-reduce.16.cloned.1.call-start = ((), (), s32[]{:S(2)}) async-start(), calls=%async_computation.2 | async-start | bytes 917504 | tf_op jit(solution)/shard_map/psum | solution.py:208
  8.1 161.7 %copy-start.31 = (f32[32]{0:T(128)}, f32[32]{0:T(128)S(1)}, u32[]{:S(2)}) copy-start(f32[32]{0:T(128)S(1)} %multiply_exponential_fusion) | copy-start | bytes 388
  53.6 116.2 %copy-start.17 = (f32[896]{0:T(1024)}, f32[896]{0:T(1024)S(1)}, u32[]{:S(2)}) copy-start(f32[896]{0:T(1024)S(1)} %convert_element_type.145) | copy-start | bytes 10756
  54.7 115.1 %copy-start.26 = (f32[128]{0:T(128)}, f32[128]{0:T(128)S(1)}, u32[]{:S(2)}) copy-start(f32[128]{0:T(128)S(1)} %add_rsqrt_fusion.1) | copy-start | bytes 1540
  97.9 71.9 %copy-start.28 = (f32[128]{0:T(128)}, f32[128]{0:T(128)S(1)}, u32[]{:S(2)}) copy-start(f32[128]{0:T(128)S(1)} %get-tuple-element.354) | copy-start | bytes 1540
  98.7 71.2 %copy-start.19 = (f32[128,32]{0,1:T(8,128)}, f32[128,32]{0,1:T(8,128)S(1)}, u32[]{:S(2)}) copy-start(f32[128,32]{0,1:T(8,128)S(1)} %get-tuple-element.375) | copy-start | bytes 49156
  226.4 123.8 %all-gather.4.cloned.1.call-start = ((), (), s32[]{:S(2)}) async-start(), calls=%async_computation.3 | async-start | bytes 4630528 | tf_op jit(solution)/shard_map/all_gather | solution.py:114
  227.0 190.4 %all-gather.6.cloned.1.call-start = ((), (), s32[]{:S(2)}) async-start(), calls=%async_computation.4 | async-start | bytes 4630528 | tf_op jit(solution)/shard_map/all_gather | solution.py:115
  227.6 267.9 %all-gather.8.cloned.1.call-start = ((), (), s32[]{:S(2)}) async-start(), calls=%async_computation.5 | async-start | bytes 4630528 | tf_op jit(solution)/shard_map/all_gather | solution.py:226
  227.6 6.5 collective-permute-start
  228.6 298.4 %all-reduce.18.cloned.1.call-start = ((), (), s32[]{:S(2)}) async-start(), calls=%async_computation.6 | async-start | bytes 458752 | tf_op jit(solution)/shard_map/psum | solution.py:241
  234.2 65.5 %copy-start.7 = (bf16[2432,56]{0,1:T(8,128)(2,1)}, bf16[2432,56]{0,1:T(8,128)(2,1)S(1)}, u32[]{:S(2)}) copy-start(bf16[2432,56]{0,1:T(8,128)(2,1)S(1)} %collective-permute-done) | copy-start | bytes 817156
  234.2 21.9 %collective-permute-start.1 = (bf16[2432,112]{0,1:T(8,128)(2,1)S(1)}, bf16[2432,112]{0,1:T(8,128)(2,1)S(1)}, u32[]{:S(2)}, u32[]{:S(2)}) collective-permute-start(bf16[2432,112]{0,1:T(8,128)(2,1)S(1)} %pad_maximum_fusion.2), channel_id=1, source_target_pairs={{0,28},{2,30},{4,0},{6,2},{8,4},{10,6},{12,8},{14,10},{16,12},{18,... | collective-permute-start | bytes 1634312 | tf_op jit(solution)/shard_map/ppermute | solution.py:22
  256.2 39.8 %collective-permute-start.2 = (bf16[2432,224]{0,1:T(8,128)(2,1)S(1)}, bf16[2432,224]{0,1:T(8,128)(2,1)S(1)}, u32[]{:S(2)}, u32[]{:S(2)}) collective-permute-start(bf16[2432,224]{0,1:T(8,128)(2,1)S(1)} %pad_maximum_fusion.1), channel_id=1, source_target_pairs={{0,24},{2,26},{4,28},{6,30},{8,0},{10,2},{12,4},{14,6},{16,8},{18,... | collective-permute-start | bytes 3268616 | tf_op jit(solution)/shard_map/ppermute | solution.py:22
  297.6 42.9 %collective-permute-start.3 = (bf16[2432,448]{0,1:T(8,128)(2,1)}, bf16[2432,448]{0,1:T(8,128)(2,1)}, u32[]{:S(2)}, u32[]{:S(2)}) collective-permute-start(bf16[2432,448]{0,1:T(8,128)(2,1)} %pad_maximum_fusion), channel_id=1, source_target_pairs={{0,16},{2,18},{4,20},{6,22},{8,24},{10,26},{12,28},{14,30},{16,0},... | collective-permute-start | bytes 6537224 | tf_op jit(solution)/shard_map/ppermute | solution.py:22
  354.4 141.1 %copy-start.13 = (bf16[1,128,896]{2,1,0:T(8,128)(2,1)S(1)}, bf16[1,128,896]{2,1,0:T(8,128)(2,1)}, u32[]{:S(2)}) copy-start(bf16[1,128,896]{2,1,0:T(8,128)(2,1)} %param.20) | copy-start | bytes 688132
  510.1 91.4 %reduce-scatter.8.cloned.1.call-start = ((), (), s32[]{:S(2)}) async-start(), calls=%async_computation.7 | async-start | bytes 294912
  538.0 97.6 %all-reduce.20.cloned.1.call-start = ((), (), s32[]{:S(2)}) async-start(), calls=%async_computation.9 | async-start | bytes 917504 | tf_op jit(solution)/shard_map/psum | solution.py:216
  538.3 64.2 %copy-start.29 = (f32[128]{0:T(128)S(1)}, f32[128]{0:T(128)}, u32[]{:S(2)}) copy-start(f32[128]{0:T(128)} %copy-done.28) | copy-start | bytes 1540
  538.3 64.4 %copy-start.15 = (bf16[896,128]{1,0:T(8,128)(2,1)S(1)}, bf16[896,128]{1,0:T(8,128)(2,1)}, u32[]{:S(2)}) copy-start(bf16[896,128]{1,0:T(8,128)(2,1)} %copy-done.14) | copy-start | bytes 688132
  604.7 341.1 %reduce-scatter.10.cloned.1.call-start = ((), (), s32[]{:S(2)}) async-start(), calls=%async_computation.8 | async-start | bytes 15841280
  (26 other events, 531.9 us)
Sparse Core Ops, SparseCore 0:
  226.5 15.8 all-reduce.15
  510.2 16.7 all-reduce.17
  538.1 63.2 reduce-scatter.7
  604.8 17.6 all-reduce.19
Sparse Core Ops, SparseCore 1:
  229.7 108.7 all-gather.3
  341.1 76.2 all-gather.5
  420.1 75.3 all-gather.7
  635.0 310.8 reduce-scatter.9
